TPU v7x, 128 devices: a whole 4x4x4 slice. The times are simulated.
128 devices in a mesh: dp: 16 (over z, y), vocab: 8 (over x, core).
Axes of the slice: x: 4, y: 4, z: 4, core: 2. Of those that a mesh axis runs over, the one named last changes fastest.
Arguments:
- hidden: bfloat16 [32, 512, 1024], P('dp'), may hold values from -24 to 24
- norm_gain: float32 [1024], replicated, may hold values from 0.5 to 1.5
- head: bfloat16 [1024, 32000], P('dp', 'vocab'), may hold values from -4 to 4
- targets: int32 [32, 512], P('dp'), may hold values from 0 to 31999
- lengths: int32 [32], P('dp'), may hold values from 1 to 512, 9216 in all
- groups: int32 [32, 1], P('dp'), may hold values from 0 to 3
- baseline: float32 [4], replicated, may hold values from -2 to 0
Outputs:
- logprob: float32 [32, 512], P('dp')
- entropy: float32 [32, 512], P('dp')
- group_shift: float32 [2, 4], replicated
Inputs may be any that keep to these rules, and one draw needn't show every extreme that they name: `groups`: every group holds at least one sequence.
All inputs are finite; a program needn't handle non-finite values. No bound on the sum of `lengths` on one device may be relied on, other than what follows from the above.
Results may differ from a plain program's by a relative error of at most 0.00045.
The roundings to bfloat16 on the way count: a program that leaves them out, or rounds other values in their place, can miss the bound.
Values may be sent and summed in bfloat16 or wider, within the bound.
No kernel may reach another device: no remote copies, remote signals or barrier semaphores. Data moves between devices by JAX's collectives and lax.ppermute only.
A program may use at most 64 MiB of HBM per device.

v0:
```python
import jax
import jax.numpy as jnp
from jax import lax
from jax.sharding import PartitionSpec as P


def per_device(hidden, norm_gain, head, targets, lengths, groups, baseline):
    seq_count, slot_count, width = hidden.shape
    total_rows = seq_count * slot_count
    block = min(512, total_rows)
    weights = lax.all_gather(head, "dp", axis=0, tiled=True)
    vocab_width = weights.shape[1]
    offset = lax.axis_index("vocab") * vocab_width
    flat = hidden.reshape(total_rows, width).astype(jnp.float32)
    square = jnp.mean(flat * flat, axis=-1, keepdims=True)
    normed = (flat * lax.rsqrt(square + 1e-05) * norm_gain[None, :]).astype(jnp.bfloat16)
    positions = jnp.arange(slot_count, dtype=jnp.int32)
    live = (positions[None, :] < lengths[:, None]).reshape(total_rows)
    wanted = targets.reshape(total_rows)
    column = jnp.arange(vocab_width, dtype=jnp.int32) + offset

    def score(rows, picks):
        logits = jnp.dot(rows, weights, preferred_element_type=jnp.float32)
        local_top = jnp.max(logits, axis=-1)
        shifted = logits - local_top[:, None]
        expo = jnp.exp(shifted)
        local_total = jnp.sum(expo, axis=-1)
        local_spread = jnp.sum(expo * shifted, axis=-1)
        chosen = jnp.sum(jnp.where(column[None, :] == picks[:, None], logits, 0.0), axis=-1)
        top = lax.pmax(local_top, "vocab")
        factor = jnp.exp(local_top - top)
        total, spread, target = lax.psum(
            (
                local_total * factor,
                factor * (local_spread + local_total * (local_top - top)),
                chosen,
            ),
            "vocab",
        )
        return (target - top - jnp.log(total), jnp.log(total) - spread / total)

    blocks = (total_rows + block - 1) // block

    def advance(index, carry):
        out_lp, out_ent = carry
        start = index * block
        part_rows = lax.dynamic_slice_in_dim(normed, start, block, 0)
        part_picks = lax.dynamic_slice_in_dim(wanted, start, block, 0)
        block_lp, block_ent = score(part_rows, part_picks)
        out_lp = lax.dynamic_update_slice_in_dim(out_lp, block_lp, start, 0)
        out_ent = lax.dynamic_update_slice_in_dim(out_ent, block_ent, start, 0)
        return (out_lp, out_ent)

    empty = jnp.zeros((normed.shape[0],), jnp.float32)
    logprob, entropy = lax.fori_loop(0, blocks, advance, (empty, empty))
    logprob = jnp.where(live, logprob, 0.0).reshape(seq_count, slot_count)
    entropy = jnp.where(live, entropy, 0.0).reshape(seq_count, slot_count)
    group_count = baseline.shape[0]
    member = (groups[:, 0][:, None] == jnp.arange(group_count, dtype=jnp.int32)[None, :]).astype(
        jnp.float32
    )
    seq_sums = jnp.stack(
        [jnp.sum(logprob, axis=1), jnp.sum(entropy, axis=1), lengths.astype(jnp.float32)], axis=1
    )
    partial_value = jnp.dot(member.T, seq_sums, precision=lax.Precision.HIGHEST)
    group_lp, group_ent, group_cnt = lax.psum(
        (partial_value[:, 0], partial_value[:, 1], partial_value[:, 2]), "dp"
    )
    shift = jnp.stack([group_lp / group_cnt - baseline, group_ent / group_cnt], axis=0)
    return (logprob, entropy, shift)


def solution(mesh):
    placed = (
        P("dp", None, None),
        P(),
        P("dp", "vocab"),
        P("dp", None),
        P("dp"),
        P("dp", None),
        P(),
    )
    return jax.shard_map(
        per_device,
        mesh=mesh,
        in_specs=placed,
        out_specs=(P("dp", None), P("dp", None), P()),
        check_vma=False,
    )
```

profile of v0, /device:TPU:0, one launch (start us, length us, event | category | flops | bytes accessed | tf_op | source)
XLA Modules:
  0.0 203.4 jit_solution(1171368510043875422)
XLA Ops:
  7.2 0.0 all-gather.2.cloned.1.call-start
  7.2 0.7 all-gather.2.cloned.1.call-update
  7.9 2.1 %multiply_reduce_fusion = f32[2,512]{1,0:T(2,128)S(1)} fusion(bf16[2,512,1024]{2,1,0:T(8,128)(2,1)} %param.9), kind=kLoop, calls=%fused_computation.16 | loop fusion | flops 3144704 | bytes 2101248 | tf_op jit(solution)/shard_map/reduce_sum | solution.py:15
  10.0 0.7 copy.10
  10.7 0.7 iota_compare_fusion
  11.4 0.7 convert_bitcast_fusion
  12.1 2.1 %fusion.7 = bf16[1024,1024]{1,0:T(8,128)(2,1)S(1)} fusion(f32[1024]{0:T(1024)} %param.10, f32[1024]{0:T(1024)S(1)} %bitcast.30, bf16[2,512,1024]{2,1,0:T(8,128)(2,1)} %param.9), kind=kLoop, calls=%fused_computation.15 | loop fusion | flops 4194304 | bytes 4202496 | tf_op jit(solution)/shard_map/convert_element_type | solution.py:16
  14.3 69.3 %all-gather.2.cloned.1.call-done = bf16[1024,4000]{1,0:T(8,128)(2,1)} async-done(((bf16[64,4000]{1,0:T(8,128)(2,1)}), bf16[1024,4000]{1,0:T(8,128)(2,1)}) %all-gather.2.cloned.1.call-update) | async-done | bytes 8192016 | tf_op jit(solution)/shard_map/all_gather | solution.py:11
  83.6 73.4 %while.16 = (s32[]{:T(128)}, f32[1024]{0:T(1024)S(1)}, f32[1024]{0:T(1024)S(1)}, s32[1024]{0:T(1024)S(1)}, bf16[1024,1024]{1,0:T(8,128)(2,1)S(1)}, /*index=5*/bf...) while((s32[]{:T(128)}, f32[1024]{0:T(1024)S(1)}, ...), condition=%wide.region_10.11_spmd.clone, body=%wide.region_1.10_spmd.clone.sunk | while | flops 4210696704 | bytes 25714092 | solution.py:55
  83.6 7.1 %fusion.24 = (f32[512]{0:T(512)S(1)}, f32[512,4000]{0,1:T(8,128)S(1)}) fusion(bf16[1024,4000]{1,0:T(8,128)(2,1)} %get-tuple-element.277, bf16[1024,1024]{1,0:T(8,128)(2,1)S(1)} %get-tuple-element.276, s32[]{:T(128)S(6)} %select_n.33), kind=kOutput, calls=%fused_computation.38.clone.1 | convolution fusion | flops 4196351488 | bytes 17434628 | tf_op jit(solution)/shard_map/while/body/eval_jaxpr/dot_general | solution.py:23
  90.7 0.1 dynamic_slice.23
  90.8 3.2 %fusion.25 = (f32[512]{0:T(512)S(1)}, f32[512]{0:T(512)S(1)}, f32[512]{0:T(512)S(1)}) fusion(f32[512,4000]{0,1:T(8,128)S(1)} %get-tuple-element.238, f32[512]{0:T(512)S(1)} %get-tuple-element.239, s32[512]{0:T(512)S(1)} %dynamic_slice.23, s32[4000]{0:T(1024)S(1)} %iota_add_fusion.2), kind=kLoop, calls=%fused_computation.3.clone.1 | loop fusion | flops 14334464 | bytes 8218240 | tf_op jit(solution)/shard_map/while/body/eval_jaxpr/reduce_sum | solution.py:28
  94.1 14.4 %pmax.13 = f32[512]{0:T(512)S(1)} all-reduce(f32[512]{0:T(512)S(1)} %get-tuple-element.239), channel_id=1, replica_groups=mesh['dp'=16,'vocab'=8] {'vocab'}, use_global_device_ids=true, to_apply=%region_5.5 | all-reduce | flops 512 | bytes 4096 | tf_op jit(solution)/shard_map/while/body/eval_jaxpr/pmax | solution.py:30
  108.5 12.6 %all-reduce.3 = (f32[512]{0:T(512)S(1)}, f32[512]{0:T(512)S(1)}, f32[512]{0:T(512)S(1)}) all-reduce(f32[512]{0:T(512)S(1)} %get-tuple-element.240, f32[512]{0:T(512)S(1)} %get-tuple-element.243, f32[512]{0:T(512)S(1)} %get-tuple-element.244), channel_id=1, replica_groups=mesh['dp'=16,'vocab'=8] {'vocab'}, use_global_device_ids=true, to_apply=%region_3.0 | all-reduce | flops 1536 | bytes 12288 | tf_op jit(solution)/shard_map/while/body/eval_jaxpr/psum | solution.py:32
  121.1 0.1 subtract_dynamic-update-slice_fusion.3
  121.3 7.1 %fusion.24 = (f32[512]{0:T(512)S(1)}, f32[512,4000]{0,1:T(8,128)S(1)}) fusion(bf16[1024,4000]{1,0:T(8,128)(2,1)} %get-tuple-element.277, bf16[1024,1024]{1,0:T(8,128)(2,1)S(1)} %get-tuple-element.276, s32[]{:T(128)S(6)} %select_n.33), kind=kOutput, calls=%fused_computation.38.clone.1 | convolution fusion | flops 4196351488 | bytes 17434628 | tf_op jit(solution)/shard_map/while/body/eval_jaxpr/dot_general | solution.py:23
  128.4 0.1 dynamic_slice.23
  128.5 3.2 %fusion.25 = (f32[512]{0:T(512)S(1)}, f32[512]{0:T(512)S(1)}, f32[512]{0:T(512)S(1)}) fusion(f32[512,4000]{0,1:T(8,128)S(1)} %get-tuple-element.238, f32[512]{0:T(512)S(1)} %get-tuple-element.239, s32[512]{0:T(512)S(1)} %dynamic_slice.23, s32[4000]{0:T(1024)S(1)} %iota_add_fusion.2), kind=kLoop, calls=%fused_computation.3.clone.1 | loop fusion | flops 14334464 | bytes 8218240 | tf_op jit(solution)/shard_map/while/body/eval_jaxpr/reduce_sum | solution.py:28
  131.7 12.4 %pmax.13 = f32[512]{0:T(512)S(1)} all-reduce(f32[512]{0:T(512)S(1)} %get-tuple-element.239), channel_id=1, replica_groups=mesh['dp'=16,'vocab'=8] {'vocab'}, use_global_device_ids=true, to_apply=%region_5.5 | all-reduce | flops 512 | bytes 4096 | tf_op jit(solution)/shard_map/while/body/eval_jaxpr/pmax | solution.py:30
  144.2 12.6 %all-reduce.3 = (f32[512]{0:T(512)S(1)}, f32[512]{0:T(512)S(1)}, f32[512]{0:T(512)S(1)}) all-reduce(f32[512]{0:T(512)S(1)} %get-tuple-element.240, f32[512]{0:T(512)S(1)} %get-tuple-element.243, f32[512]{0:T(512)S(1)} %get-tuple-element.244), channel_id=1, replica_groups=mesh['dp'=16,'vocab'=8] {'vocab'}, use_global_device_ids=true, to_apply=%region_3.0 | all-reduce | flops 1536 | bytes 12288 | tf_op jit(solution)/shard_map/while/body/eval_jaxpr/psum | solution.py:32
  156.8 0.1 subtract_dynamic-update-slice_fusion.3
  157.0 0.0 copy-start
  157.0 0.0 copy-start.1
  157.0 0.1 reduce_sum.67
  157.1 0.1 reduce_sum.68
  157.3 0.0 copy-done.3
  157.3 0.2 fusion.8
  157.5 38.5 %all-reduce.1 = (f32[4]{0:T(128)S(1)}, f32[4]{0:T(128)S(1)}, f32[4]{0:T(128)S(1)}) all-reduce(f32[4]{0:T(128)S(1)} %get-tuple-element.177, f32[4]{0:T(128)S(1)} %get-tuple-element.178, f32[4]{0:T(128)S(1)} %get-tuple-element.176), channel_id=1, replica_groups=mesh['dp'=16,'vocab'=8] {'dp'}, use_global_device_ids=true, to_apply=%region_15.16 | all-reduce | flops 12 | bytes 96 | tf_op jit(solution)/shard_map/psum | solution.py:66
  195.9 0.0 copy-done.2
  195.9 0.6 pad_maximum_fusion
  196.5 0.0 copy-done
  196.5 0.0 copy-done.1
  (16 shorter events, 0.1 us)
Async XLA Ops:
  7.2 76.4 %all-gather.2.cloned.1.call-start = ((), (), s32[]{:S(2)}) async-start(), calls=%async_computation | async-start | bytes 8912896 | tf_op jit(solution)/shard_map/all_gather | solution.py:11
  83.6 73.7 %copy-start.3 = (s32[2,1]{0,1:T(1,128)S(1)}, s32[2,1]{0,1:T(1,128)}, u32[]{:S(2)}) copy-start(s32[2,1]{0,1:T(1,128)} %param.14) | copy-start | bytes 28
  83.6 112.3 %copy-start.2 = (f32[4]{0:T(128)S(1)}, f32[4]{0:T(128)}, u32[]{:S(2)}) copy-start(f32[4]{0:T(128)} %param.15) | copy-start | bytes 52
  157.0 39.5 %copy-start = (f32[2,512]{1,0:T(2,128)}, f32[2,512]{1,0:T(2,128)S(1)}, u32[]{:S(2)}) copy-start(f32[2,512]{1,0:T(2,128)S(1)} %reshape.45) | copy-start | bytes 12292
  157.0 39.5 %copy-start.1 = (f32[2,512]{1,0:T(2,128)}, f32[2,512]{1,0:T(2,128)S(1)}, u32[]{:S(2)}) copy-start(f32[2,512]{1,0:T(2,128)S(1)} %reshape.46) | copy-start | bytes 12292
Sparse Core Ops, SparseCore 0:
  10.1 73.4 all-gather.1
where the time goes:
time: 204 us; the launch traced here: 203 us
  blocking collectives  90.5 us (44%)
  waiting for transfers between devices  70 us (34%)
  matrix products  14.4 us (7%)
  between operations  14.1 us (7%)
  other arithmetic  13.3 us (7%)
    all_gather x1, waiting for transfers between devices, per_device(): weights = lax.all_gather(head, 'dp', axis=0, tiled=True)  69.3 us
    psum x1, blocking collectives, per_device(): lax.psum((partial_value[:, 0], partial_value[:, 1], partial_value[:, 2]),...  38.5 us
    pmax x2, blocking collectives, score(): top = lax.pmax(local_top, 'vocab')  26.8 us
    psum x2, blocking collectives, score(): lax.psum((local_total * factor, factor * (local_spread + local_total * (l...  25.3 us
    dot_general x2, matrix products, score(): logits = jnp.dot(rows, weights, preferred_element_type=jnp.float32)  14.3 us
    reduce_sum x2, other arithmetic, score(): local_spread = jnp.sum(expo * shifted, axis=-1)  6.5 us
  transfers between devices with their start and end apart: 1, of which 1 were waited for; matrix products, arithmetic and copies ran while one was open for 3% of the time, Pallas kernels for 0%

commit v1 on v0

--- a/solution.py
+++ b/solution.py
@@ -8,7 +8,9 @@
     seq_count, slot_count, width = hidden.shape
     total_rows = seq_count * slot_count
     block = min(512, total_rows)
-    weights = lax.all_gather(head, "dp", axis=0, tiled=True)
+    weights = jnp.concatenate(
+        lax.all_to_all(jnp.stack([head] * lax.axis_size("dp")), "dp", 0, 0), axis=0
+    )
     vocab_width = weights.shape[1]
     offset = lax.axis_index("vocab") * vocab_width
     flat = hidden.reshape(total_rows, width).astype(jnp.float32)

time: 204 us -> 250 us (1.23)
  waiting for transfers between devices: 70 us -> 122 us
  between operations: 14.1 us -> 0.74 us
  starting transfers between devices: 0.04 us -> 8.35 us
  local copies, waits for them, and re-layouts: 0.92 us -> 5.57 us
  other arithmetic: 13.3 us -> 10.1 us
    all_to_all x0 -> x1, waiting for transfers between devices: none -> 122 us  [per_device(): lax.all_to_all(jnp.stack([head] * lax.axis_size('dp')), 'dp', 0, 0)]
    all_gather x1 -> x0, waiting for transfers between devices: 69.3 us -> none  [per_device(): weights = lax.all_gather(head, 'dp', axis=0, tiled=True)]
    all_to_all x0 -> x1, starting transfers between devices: none -> 8.35 us  [per_device(): lax.all_to_all(jnp.stack([head] * lax.axis_size('dp')), 'dp', 0, 0)]
    another operation x0 -> x1, local copies, waits for them, and re-layouts: none -> 5.33 us  [per_device(): jnp.stack([head] * lax.axis_size('dp'))]
  transfers between devices with their start and end apart: 1 -> 1, of which waited for: 1 -> 1; matrix products, arithmetic and copies ran while one was open for 3% -> 1% of each run, Pallas kernels for 0% -> 0%
where the time goes in v1:
time: 250 us
  waiting for transfers between devices  122 us (49%)
  blocking collectives  88.5 us (35%)
  matrix products  15.1 us (6%)
  other arithmetic  10.1 us (4%)
  starting transfers between devices  8.35 us (3%)
  local copies, waits for them, and re-layouts  5.57 us (2%)
    all_to_all x1, waiting for transfers between devices, per_device(): lax.all_to_all(jnp.stack([head] * lax.axis_size('dp')), 'dp', 0, 0)  122 us
    psum x1, blocking collectives, per_device(): lax.psum((partial_value[:, 0], partial_value[:, 1], partial_value[:, 2]),...  37.3 us
    pmax x2, blocking collectives, score(): top = lax.pmax(local_top, 'vocab')  25.9 us
    psum x2, blocking collectives, score(): lax.psum((local_total * factor, factor * (local_spread + local_total * (l...  25.3 us
    dot_general x2, matrix products, score(): logits = jnp.dot(rows, weights, preferred_element_type=jnp.float32)  14.9 us
    all_to_all x1, starting transfers between devices, per_device(): lax.all_to_all(jnp.stack([head] * lax.axis_size('dp')), 'dp', 0, 0)  8.35 us
    reduce_sum x2, other arithmetic, score(): local_spread = jnp.sum(expo * shifted, axis=-1)  6.47 us
    another operation x1, local copies, waits for them, and re-layouts, per_device(): jnp.stack([head] * lax.axis_size('dp'))  5.33 us
  transfers between devices with their start and end apart: 1, of which 1 were waited for; matrix products, arithmetic and copies ran while one was open for 1% of the time, Pallas kernels for 0%

profile of v1, /device:TPU:0, one launch (start us, length us, event | category | flops | bytes accessed | tf_op | source)
XLA Modules:
  0.0 250.1 jit_solution(11141085017558665829)
XLA Ops:
  0.6 5.3 %stack.16 = bf16[16,64,4000]{2,1,0:T(8,128)(2,1)} broadcast(bf16[64,4000]{1,0:T(8,128)(2,1)} %param.11), dimensions={1,2} | broadcast | bytes 8704000 | tf_op jit(solution)/shard_map/stack | solution.py:12
  6.0 8.4 %all-to-all-start = ((bf16[16,64,4000]{2,1,0:T(8,128)(2,1)}), bf16[16,64,4000]{2,1,0:T(8,128)(2,1)}, u32[]{:S(2)}, u32[]{:S(2)}) async-start(bf16[16,64,4000]{2,1,0:T(8,128)(2,1)} %stack.16), calls=%async_computation | async-start | bytes 16777216 | tf_op jit(solution)/shard_map/all_to_all | solution.py:12
  14.3 0.0 copy-done
  14.3 0.5 multiply_reduce_fusion
  14.9 0.0 copy-done.3
  14.9 0.0 copy-done.5
  14.9 0.1 iota_compare_fusion
  15.0 0.0 copy-done.4
  15.0 1.9 fusion.7
  16.9 121.6 %all-to-all-done = bf16[16,64,4000]{2,1,0:T(8,128)(2,1)} async-done(((bf16[16,64,4000]{2,1,0:T(8,128)(2,1)}), bf16[16,64,4000]{2,1,0:T(8,128)(2,1)}, u32[]{:S(2)}, u32[]{:S(2)}) %all-to-all-start) | async-done | bytes 8192032 | tf_op jit(solution)/shard_map/all_to_all | solution.py:12
  138.5 73.1 %while.16 = (s32[]{:T(128)}, f32[1024]{0:T(1024)S(1)}, f32[1024]{0:T(1024)S(1)}, s32[1024]{0:T(1024)S(1)}, bf16[1024,1024]{1,0:T(8,128)(2,1)}, /*index=5*/bf16[1...) while((s32[]{:T(128)}, f32[1024]{0:T(1024)S(1)}, ...), condition=%wide.region_10.11_spmd.clone, body=%wide.region_1.10_spmd.clone.sunk | while | flops 4210696704 | bytes 25910700 | solution.py:57
  138.5 7.5 %fusion.24 = (f32[512]{0:T(512)S(1)}, f32[512,4000]{0,1:T(8,128)S(1)}) fusion(bf16[1024,4000]{1,0:T(8,128)(2,1)} %get-tuple-element.277, bf16[1024,1024]{1,0:T(8,128)(2,1)} %get-tuple-element.276, s32[]{:T(128)S(6)} %select_n.33), kind=kOutput, calls=%fused_computation.38.clone.1 | convolution fusion | flops 4196351488 | bytes 17631236 | tf_op jit(solution)/shard_map/while/body/eval_jaxpr/dot_general | solution.py:25
  146.0 0.1 dynamic_slice.23
  146.1 3.2 %fusion.25 = (f32[512]{0:T(512)S(1)}, f32[512]{0:T(512)S(1)}, f32[512]{0:T(512)S(1)}) fusion(f32[512,4000]{0,1:T(8,128)S(1)} %get-tuple-element.238, f32[512]{0:T(512)S(1)} %get-tuple-element.239, s32[512]{0:T(512)S(1)} %dynamic_slice.23, s32[4000]{0:T(1024)S(1)} %iota_add_fusion.2), kind=kLoop, calls=%fused_computation.3.clone.1 | loop fusion | flops 14334464 | bytes 8218240 | tf_op jit(solution)/shard_map/while/body/eval_jaxpr/reduce_sum | solution.py:30
  149.3 13.5 %pmax.13 = f32[512]{0:T(512)S(1)} all-reduce(f32[512]{0:T(512)S(1)} %get-tuple-element.239), channel_id=1, replica_groups=mesh['dp'=16,'vocab'=8] {'vocab'}, use_global_device_ids=true, to_apply=%region_5.5 | all-reduce | flops 512 | bytes 4096 | tf_op jit(solution)/shard_map/while/body/eval_jaxpr/pmax | solution.py:32
  162.8 12.6 %all-reduce.3 = (f32[512]{0:T(512)S(1)}, f32[512]{0:T(512)S(1)}, f32[512]{0:T(512)S(1)}) all-reduce(f32[512]{0:T(512)S(1)} %get-tuple-element.240, f32[512]{0:T(512)S(1)} %get-tuple-element.243, f32[512]{0:T(512)S(1)} %get-tuple-element.244), channel_id=1, replica_groups=mesh['dp'=16,'vocab'=8] {'vocab'}, use_global_device_ids=true, to_apply=%region_3.0 | all-reduce | flops 1536 | bytes 12288 | tf_op jit(solution)/shard_map/while/body/eval_jaxpr/psum | solution.py:34
  175.5 0.1 subtract_dynamic-update-slice_fusion.3
  175.6 7.5 %fusion.24 = (f32[512]{0:T(512)S(1)}, f32[512,4000]{0,1:T(8,128)S(1)}) fusion(bf16[1024,4000]{1,0:T(8,128)(2,1)} %get-tuple-element.277, bf16[1024,1024]{1,0:T(8,128)(2,1)} %get-tuple-element.276, s32[]{:T(128)S(6)} %select_n.33), kind=kOutput, calls=%fused_computation.38.clone.1 | convolution fusion | flops 4196351488 | bytes 17631236 | tf_op jit(solution)/shard_map/while/body/eval_jaxpr/dot_general | solution.py:25
  183.1 0.1 dynamic_slice.23
  183.2 3.2 %fusion.25 = (f32[512]{0:T(512)S(1)}, f32[512]{0:T(512)S(1)}, f32[512]{0:T(512)S(1)}) fusion(f32[512,4000]{0,1:T(8,128)S(1)} %get-tuple-element.238, f32[512]{0:T(512)S(1)} %get-tuple-element.239, s32[512]{0:T(512)S(1)} %dynamic_slice.23, s32[4000]{0:T(1024)S(1)} %iota_add_fusion.2), kind=kLoop, calls=%fused_computation.3.clone.1 | loop fusion | flops 14334464 | bytes 8218240 | tf_op jit(solution)/shard_map/while/body/eval_jaxpr/reduce_sum | solution.py:30
  186.4 12.4 %pmax.13 = f32[512]{0:T(512)S(1)} all-reduce(f32[512]{0:T(512)S(1)} %get-tuple-element.239), channel_id=1, replica_groups=mesh['dp'=16,'vocab'=8] {'vocab'}, use_global_device_ids=true, to_apply=%region_5.5 | all-reduce | flops 512 | bytes 4096 | tf_op jit(solution)/shard_map/while/body/eval_jaxpr/pmax | solution.py:32
  198.8 12.6 %all-reduce.3 = (f32[512]{0:T(512)S(1)}, f32[512]{0:T(512)S(1)}, f32[512]{0:T(512)S(1)}) all-reduce(f32[512]{0:T(512)S(1)} %get-tuple-element.240, f32[512]{0:T(512)S(1)} %get-tuple-element.243, f32[512]{0:T(512)S(1)} %get-tuple-element.244), channel_id=1, replica_groups=mesh['dp'=16,'vocab'=8] {'vocab'}, use_global_device_ids=true, to_apply=%region_3.0 | all-reduce | flops 1536 | bytes 12288 | tf_op jit(solution)/shard_map/while/body/eval_jaxpr/psum | solution.py:34
  211.5 0.1 subtract_dynamic-update-slice_fusion.3
  211.7 0.0 copy-start.1
  211.7 0.0 copy-start.2
  211.7 0.1 reduce_sum.67
  211.8 0.1 reduce_sum.68
  211.9 0.0 copy-done.7
  211.9 0.2 fusion.8
  212.1 37.3 %all-reduce.1 = (f32[4]{0:T(128)S(1)}, f32[4]{0:T(128)S(1)}, f32[4]{0:T(128)S(1)}) all-reduce(f32[4]{0:T(128)S(1)} %get-tuple-element.177, f32[4]{0:T(128)S(1)} %get-tuple-element.178, f32[4]{0:T(128)S(1)} %get-tuple-element.176), channel_id=1, replica_groups=mesh['dp'=16,'vocab'=8] {'dp'}, use_global_device_ids=true, to_apply=%region_15.16 | all-reduce | flops 12 | bytes 96 | tf_op jit(solution)/shard_map/psum | solution.py:68
  249.5 0.0 copy-done.6
  249.5 0.6 pad_maximum_fusion
  (24 shorter events, 0.1 us)
Async XLA Ops:
  6.0 8.4 %copy-start = (bf16[2,512,1024]{2,1,0:T(8,128)(2,1)S(1)}, bf16[2,512,1024]{2,1,0:T(8,128)(2,1)}, u32[]{:S(2)}) copy-start(bf16[2,512,1024]{2,1,0:T(8,128)(2,1)} %param.9) | copy-start | bytes 6291460
  6.0 8.9 %copy-start.3 = (s32[2,512]{1,0:T(2,128)S(1)}, s32[2,512]{1,0:T(2,128)}, u32[]{:S(2)}) copy-start(s32[2,512]{1,0:T(2,128)} %param.12) | copy-start | bytes 12292
  6.0 8.9 %copy-start.5 = (s32[2]{0:T(128)S(1)}, s32[2]{0:T(128)}, u32[]{:S(2)}) copy-start(s32[2]{0:T(128)} %param.13) | copy-start | bytes 28
  6.0 9.0 %copy-start.4 = (f32[1024]{0:T(1024)S(1)}, f32[1024]{0:T(1024)}, u32[]{:S(2)}) copy-start(f32[1024]{0:T(1024)} %param.10) | copy-start | bytes 12292
  6.0 132.5 %all-to-all-start = ((bf16[16,64,4000]{2,1,0:T(8,128)(2,1)}), bf16[16,64,4000]{2,1,0:T(8,128)(2,1)}, u32[]{:S(2)}, u32[]{:S(2)}) async-start(bf16[16,64,4000]{2,1,0:T(8,128)(2,1)} %stack.16), calls=%async_computation | async-start | bytes 16777216 | tf_op jit(solution)/shard_map/all_to_all | solution.py:12
  138.5 73.5 %copy-start.7 = (s32[2,1]{0,1:T(1,128)S(1)}, s32[2,1]{0,1:T(1,128)}, u32[]{:S(2)}) copy-start(s32[2,1]{0,1:T(1,128)} %param.14) | copy-start | bytes 28
  138.5 111.0 %copy-start.6 = (f32[4]{0:T(128)S(1)}, f32[4]{0:T(128)}, u32[]{:S(2)}) copy-start(f32[4]{0:T(128)} %param.15) | copy-start | bytes 52
  211.7 38.4 %copy-start.1 = (f32[2,512]{1,0:T(2,128)}, f32[2,512]{1,0:T(2,128)S(1)}, u32[]{:S(2)}) copy-start(f32[2,512]{1,0:T(2,128)S(1)} %reshape.51) | copy-start | bytes 12292
  211.7 38.4 %copy-start.2 = (f32[2,512]{1,0:T(2,128)}, f32[2,512]{1,0:T(2,128)S(1)}, u32[]{:S(2)}) copy-start(f32[2,512]{1,0:T(2,128)S(1)} %reshape.52) | copy-start | bytes 12292
